TPU v7x, 32 devices: a whole 2x2x4 slice. The times are simulated.
32 devices in a mesh: req: 8 (over z, x), tp: 4 (over y, core).
Axes of the slice: x: 2, y: 2, z: 4, core: 2. Of those that a mesh axis runs over, the one named last changes fastest.
Arguments:
- hidden_in: bfloat16 [8, 1024, 1024], P('req', 'tp'), may hold values from -6 to 6
- short_cache: bfloat16 [8, 1536, 2, 1024], P('req', None, None, 'tp')
- long_cache: bfloat16 [3, 4096, 2, 1024], P(None, 'req', None, 'tp')
- short_len: int32 [8], P('req'), may hold values from 512 to 1536, as said below
- long_owner: int32 [3], replicated, may hold values from 0 to 7, as said below
- w_qkv: bfloat16 [3, 1024, 1024], P(None, None, 'tp'), may hold values from -0.1875 to 0.1875
- b_qkv: float32 [3, 1024], P(None, 'tp'), may hold values from -3 to 3
- w_out: bfloat16 [1024, 1024], P('tp'), may hold values from -0.1875 to 0.1875
- b_out: float32 [1024], replicated, may hold values from -3 to 3
- w_in: bfloat16 [1024, 4096], P(None, 'tp'), may hold values from -0.1875 to 0.1875
- b_in: float32 [4096], P('tp'), may hold values from -3 to 3
- w_down: bfloat16 [4096, 1024], P('tp'), may hold values from -0.09375 to 0.09375
- b_down: float32 [1024], replicated, may hold values from -3 to 3
- norm_gain: float32 [2, 1024], replicated, may hold values from 0.1 to 1.9
- norm_offset: float32 [2, 1024], replicated, may hold values from -2 to 2
Outputs:
- hidden_out: bfloat16 [8, 1024, 1024], P('req', 'tp')
- new_kv: bfloat16 [8, 1024, 2, 1024], P('req', None, None, 'tp')
Inputs may be any that keep to these rules, and one draw needn't show every extreme that they name: `short_len`: some request uses all 1536 positions. `long_owner`: 3 different requests.
All inputs are finite; a program needn't handle non-finite values.
Results may differ from a plain program's by a relative error of at most 0.025.
The roundings to bfloat16 on the way count: a program that leaves them out, or rounds other values in their place, can miss the bound.
Values may be sent and summed in bfloat16 or wider, within the bound.
No kernel may reach another device: no remote copies, remote signals or barrier semaphores. Data moves between devices by JAX's collectives and lax.ppermute only.
A program may use at most 192 MiB of HBM per device.

v0:
```python
import jax
import jax.numpy as jnp
from jax import lax
from jax.sharding import PartitionSpec as P

HEAD_DIM = 64


masked_score = -1e30


def layer_norm(rows_in, gain, shift):
    center = rows_in - jnp.mean(rows_in, axis=-1, keepdims=True)
    spread = jnp.mean(center * center, axis=-1, keepdims=True)
    return center * lax.rsqrt(spread + 1e-05) * gain + shift


def partial_attend(query_matrix, key_matrix, value_matrix, allowed):
    logit_scores = jnp.einsum(
        "wux,jux->uwj", query_matrix, key_matrix, preferred_element_type=jnp.float32
    )
    logit_scores = jnp.where(allowed[None], logit_scores, masked_score)
    row_peak = jnp.max(logit_scores, axis=2)
    softmax_weights = jnp.where(allowed[None], jnp.exp(logit_scores - row_peak[:, :, None]), 0.0)
    row_total = jnp.sum(softmax_weights, axis=2)
    summed = jnp.einsum(
        "rij,jrx->irx",
        softmax_weights.astype(jnp.bfloat16),
        value_matrix,
        preferred_element_type=jnp.float32,
    )
    return (row_peak, row_total, summed.reshape(summed.shape[0], -1))


def merge_parts(first, second):
    joint_peak = jnp.maximum(first[0], second[0])
    first_scale = jnp.exp(first[0] - joint_peak)
    second_scale = jnp.exp(second[0] - joint_peak)
    joint_total = first[1] * first_scale + second[1] * second_scale
    first_wide = jnp.repeat(jnp.swapaxes(first_scale, -1, -2), HEAD_DIM, axis=-1)
    second_wide = jnp.repeat(jnp.swapaxes(second_scale, -1, -2), HEAD_DIM, axis=-1)
    return (joint_peak, joint_total, first[2] * first_wide + second[2] * second_wide)


def empty_part(head_count, row_count):
    return (
        jnp.full((head_count, row_count), masked_score, jnp.float32),
        jnp.zeros((head_count, row_count), jnp.float32),
        jnp.zeros((row_count, head_count * HEAD_DIM), jnp.float32),
    )


def attend_long(query_matrix, cache_rows):
    head_count = query_matrix.shape[1]
    block_len = min(1024, cache_rows.shape[0])
    block_count = cache_rows.shape[0] // block_len
    blocks = cache_rows.reshape(block_count, block_len, 2, head_count, HEAD_DIM)

    def fold_block(carry, piece):
        allowed = jnp.ones((1, block_len), bool)
        return (
            merge_parts(carry, partial_attend(query_matrix, piece[:, 0], piece[:, 1], allowed)),
            None,
        )

    result, unused = lax.scan(fold_block, empty_part(head_count, query_matrix.shape[0]), blocks)
    return result


def body(
    hidden_in,
    short_cache,
    long_cache,
    short_len,
    long_owner,
    w_qkv,
    b_qkv,
    w_out,
    b_out,
    w_in,
    b_in,
    w_down,
    b_down,
    norm_gain,
    norm_offset,
):
    local_rows = hidden_in[0]
    factors = jnp.array([0.125, 1.0, 1.0], jnp.float32)[None, :, None]
    mixed = jnp.einsum(
        "nd,cdk->nck",
        lax.all_gather(local_rows, "tp", axis=0, tiled=True),
        w_qkv,
        preferred_element_type=jnp.float32,
    )
    projected = ((mixed + b_qkv[None]) * factors).astype(jnp.bfloat16)
    span_len = projected.shape[0]
    head_count = projected.shape[2] // HEAD_DIM
    flat_queries = projected[:, 0]
    query_matrix = flat_queries.reshape(span_len, head_count, HEAD_DIM)
    new_keys = projected[:, 1].reshape(span_len, head_count, HEAD_DIM)
    new_values = projected[:, 2].reshape(span_len, head_count, HEAD_DIM)
    new_kv = projected[None, :, 1:3]
    short_rows = short_cache[0]
    cache_len = short_rows.shape[0]
    all_keys = jnp.concatenate(
        [short_rows[:, 0].reshape(cache_len, head_count, HEAD_DIM), new_keys], axis=0
    )
    all_values = jnp.concatenate(
        [short_rows[:, 1].reshape(cache_len, head_count, HEAD_DIM), new_values], axis=0
    )
    cache_mask = jnp.arange(cache_len) < short_len[0]
    query_block = min(512, span_len)
    block_count = span_len // query_block

    def local_block(block_index):
        first_row = block_index * query_block
        block_queries = lax.dynamic_slice_in_dim(query_matrix, first_row, query_block, 0)
        row_ids = first_row + jnp.arange(query_block)
        causal = jnp.arange(span_len)[None, :] <= row_ids[:, None]
        allowed = jnp.concatenate(
            [jnp.broadcast_to(cache_mask[None], (query_block, cache_len)), causal], axis=1
        )
        return partial_attend(block_queries, all_keys, all_values, allowed)

    block_peak, block_total, block_sums = lax.map(local_block, jnp.arange(block_count))
    resident_portion = (
        jnp.moveaxis(block_peak, 0, 1).reshape(head_count, span_len),
        jnp.moveaxis(block_total, 0, 1).reshape(head_count, span_len),
        block_sums.reshape(span_len, -1),
    )
    my_request = lax.axis_index("req")
    owned = long_owner == my_request
    has_long = jnp.any(owned)
    which_long = jnp.sum(jnp.where(owned, jnp.arange(owned.shape[0], dtype=jnp.int32), 0))
    stripes = lax.all_gather(long_cache, "req", axis=1, tiled=True)
    chosen = lax.dynamic_index_in_dim(stripes, which_long, 0, keepdims=False)
    long_part = lax.cond(
        has_long,
        lambda rows_given: attend_long(query_matrix, rows_given),
        lambda rows_given: empty_part(head_count, span_len),
        chosen,
    )
    whole = merge_parts(resident_portion, long_part)
    context = (whole[2] / jnp.repeat(whole[1].T, HEAD_DIM, axis=1)).astype(jnp.bfloat16)
    attended = (
        lax.psum_scatter(
            jnp.dot(context, w_out, preferred_element_type=jnp.float32),
            "tp",
            scatter_dimension=0,
            tiled=True,
        )
        + b_out
    )
    normed = layer_norm(
        local_rows.astype(jnp.float32) + attended, norm_gain[0], norm_offset[0]
    ).astype(jnp.bfloat16)
    units = jax.nn.gelu(
        jnp.dot(
            lax.all_gather(normed, "tp", axis=0, tiled=True),
            w_in,
            preferred_element_type=jnp.float32,
        )
        + b_in,
        approximate=False,
    ).astype(jnp.bfloat16)
    mixed = (
        lax.psum_scatter(
            jnp.dot(units, w_down, preferred_element_type=jnp.float32),
            "tp",
            scatter_dimension=0,
            tiled=True,
        )
        + b_down
    )
    hidden_out = layer_norm(
        normed.astype(jnp.float32) + mixed, norm_gain[1], norm_offset[1]
    ).astype(jnp.bfloat16)
    return (hidden_out[None], new_kv)


def solution(mesh):
    return jax.shard_map(
        body,
        mesh=mesh,
        in_specs=(
            P("req", "tp", None),
            P("req", None, None, "tp"),
            P(None, "req", None, "tp"),
            P("req"),
            P(),
            P(None, None, "tp"),
            P(None, "tp"),
            P("tp", None),
            P(),
            P(None, "tp"),
            P("tp"),
            P("tp", None),
            P(),
            P(),
            P(),
        ),
        out_specs=(P("req", "tp", None), P("req", None, None, "tp")),
        check_vma=False,
    )
```

profile of v0, /device:TPU:0, one launch (start us, length us, event | category | flops | bytes accessed | tf_op | source)
XLA Modules:
  0.0 507.7 jit_solution(2594108410382928869)
XLA Ops:
  8.0 4.9 copy.41
  14.8 6.0 %fusion.87 = (bf16[1536,1,256]{2,1,0:T(2,128)(2,1)}, bf16[1536,1,256]{2,1,0:T(2,128)(2,1)}) fusion(bf16[1536,2,256]{2,1,0:T(2,128)(2,1)} %bitcast.148), kind=kLoop, calls=%fused_computation.126 | loop fusion | bytes 3145728 | tf_op jit(solution)/shard_map/slice | solution.py:109
  24.2 4.7 copy.39
  28.9 6.0 %all-gather.9.cloned.1.call-done = bf16[1,1024,1024]{2,1,0:T(8,128)(2,1)} async-done(((bf16[1,256,1024]{2,1,0:T(8,128)(2,1)}), bf16[1,1024,1024]{2,1,0:T(8,128)(2,1)}) %all-gather.9.cloned.1.call-update) | async-done | bytes 2097168 | tf_op jit(solution)/shard_map/all_gather | solution.py:91
  41.6 55.5 %while.40 = (s32[]{:T(128)}, f32[2,4,512]{2,1,0:T(4,128)S(1)}, f32[2,4,512]{2,1,0:T(4,128)S(1)}, f32[2,512,256]{2,1,0:T(8,128)}, s32[2]{0:T(128)S(1)}, /*index=5...) while((s32[]{:T(128)}, f32[2,4,512]{2,1,0:T(4,128)S(1)}, ...), condition=%wide.region_3.4_spmd.clone, body=%wide.region_0.3_spmd.clone.sunk | while | flops 1396439040 | bytes 158675200 | solution.py:125
  44.5 5.1 select_reduce_fusion.3
  49.6 7.2 %fusion.115 = f32[4,512]{1,0:T(4,128)S(1)} fusion(f32[4,512,2560]{2,1,0:T(8,128)S(1)} %get-tuple-element.361, f32[4,512]{1,0:T(4,128)S(1)} %get-tuple-element.362, pred[512,2560]{1,0:T(8,128)(4,1)S(1)} %pad_add_fusion.2), kind=kLoop, calls=%fused_computation.4.clone.1 | loop fusion | flops 20969472 | bytes 22298624 | tf_op jit(solution)/shard_map/while/body/eval_jaxpr/reduce_sum | solution.py:25
  56.9 10.5 %fusion.116 = f32[4,512,64]{1,2,0:T(8,128)} fusion(bf16[2560,4,64]{0,2,1:T(8,128)(2,1)} %get-tuple-element.442, f32[4,512,2560]{2,1,0:T(8,128)} %copy-done.1, f32[4,512]{1,0:T(4,128)S(1)} %get-tuple-element.362, pred[512,2560]{1,0:T(8,128)(4,1)S(1)} %pad_add_fusion.2), kind=kOutput, calls=%fused_computation.5.clone.1 | convolution fusion | flops 692060160 | bytes 24125440 | tf_op jit(solution)/shard_map/while/body/eval_jaxpr/rij,jrx->irx/dot_general | solution.py:26
  72.3 4.8 select_reduce_fusion.3
  77.1 7.2 %fusion.115 = f32[4,512]{1,0:T(4,128)S(1)} fusion(f32[4,512,2560]{2,1,0:T(8,128)S(1)} %get-tuple-element.361, f32[4,512]{1,0:T(4,128)S(1)} %get-tuple-element.362, pred[512,2560]{1,0:T(8,128)(4,1)S(1)} %pad_add_fusion.2), kind=kLoop, calls=%fused_computation.4.clone.1 | loop fusion | flops 20969472 | bytes 22298624 | tf_op jit(solution)/shard_map/while/body/eval_jaxpr/reduce_sum | solution.py:25
  84.4 10.6 %fusion.116 = f32[4,512,64]{1,2,0:T(8,128)} fusion(bf16[2560,4,64]{0,2,1:T(8,128)(2,1)} %get-tuple-element.442, f32[4,512,2560]{2,1,0:T(8,128)} %copy-done.1, f32[4,512]{1,0:T(4,128)S(1)} %get-tuple-element.362, pred[512,2560]{1,0:T(8,128)(4,1)S(1)} %pad_add_fusion.2), kind=kOutput, calls=%fused_computation.5.clone.1 | convolution fusion | flops 692060160 | bytes 24125440 | tf_op jit(solution)/shard_map/while/body/eval_jaxpr/rij,jrx->irx/dot_general | solution.py:26
  97.1 116.0 %all-gather.5.cloned.1.call-done = bf16[3,4096,2,256]{1,3,2,0:T(8,128)(2,1)} async-done(((bf16[3,512,2,256]{1,3,2,0:T(8,128)(2,1)}), bf16[3,4096,2,256]{1,3,2,0:T(8,128)(2,1)}) %all-gather.5.cloned.1.call-update) | async-done | bytes 12582928 | tf_op jit(solution)/shard_map/all_gather | solution.py:135
  213.1 140.7 %conditional.1 = (f32[4,1024]{1,0:T(4,128)}, f32[4,1024]{1,0:T(4,128)}, f32[1024,256]{1,0:T(8,128)}) conditional(s32[]{:T(128)} %convert_element_type.32, () %tuple.31, (pred[3]{0:T(512)(128)(4,1)S(1)}, s32[3]{0:T(128)S(1)}, bf16[3,4096,2,256]{1,3,2,0:T(8,128)(2,1)}, bf16[1024,4,64]{0,2,1:T(8,128)(2,1)}) %tuple.108), branch_computations={%region_5.6_spmd, %region_6.12_spmd} | conditional | flops 1095794688 | bytes 94159160 | solution.py:137
  220.1 7.8 %reshape.71 = bf16[4,1024,2,4,64]{1,0,4,3,2:T(4,128)(2,1)} reshape(bf16[1,4096,2,256]{1,3,2,0:T(8,128)(2,1)} %constant_dynamic-slice_fusion) | data formatting | bytes 8388608 | tf_op jit(solution)/shard_map/cond/branch_1_fun/reshape | solution.py:57
  227.9 5.5 %copy.36 = bf16[4,1024,2,4,64]{1,4,3,2,0:T(8,128)(2,1)} copy(bf16[4,1024,2,4,64]{1,0,4,3,2:T(4,128)(2,1)} %reshape.71) | data formatting | bytes 8388608 | tf_op jit(solution)/shard_map/cond
  233.4 117.8 %while.39 = (s32[]{:T(128)}, f32[4,1024]{1,0:T(4,128)}, f32[4,1024]{1,0:T(4,128)}, f32[1024,256]{0,1:T(8,128)}, bf16[4,1024,2,4,64]{1,4,3,2,0:T(8,128)(2,1)}, /*...) while((s32[]{:T(128)}, f32[4,1024]{1,0:T(4,128)}, f32[4,1024]{1,0:T(4,128)}, ...), condition=%wide.region_11.11_spmd.clone, body=%wide.region_8.10_spmd.clone.sunk | while | flops 1095794688 | bytes 66896032 | solution.py:66
  234.7 9.2 %bitcast_reduce_fusion.2 = (f32[4,1024]{1,0:T(4,128)S(1)}, f32[4,1024,1024]{2,1,0:T(8,128)}) fusion(bf16[1024,4,64]{0,2,1:T(8,128)(2,1)} %get-tuple-element.398, bf16[1024,2,4,64]{0,3,2,1:T(8,128)(2,1)S(1)} %dynamic-slice_bitcast_fusion.2), kind=kOutput, calls=%fused_computation.20.clone.1 | convolution fusion | flops 541061120 | bytes 17842176 | tf_op jit(solution)/shard_map/cond/branch_1_fun/while/body/eval_jaxpr/wux,jux->uwj/dot_general | solution.py:19
  243.9 8.0 %fusion.120 = f32[4,1024]{1,0:T(4,128)S(1)} fusion(f32[4,1024,1024]{2,1,0:T(8,128)} %get-tuple-element.373, f32[4,1024]{1,0:T(4,128)S(1)} %get-tuple-element.371), kind=kLoop, calls=%fused_computation.23.clone.1 | loop fusion | flops 8384512 | bytes 16809984 | tf_op jit(solution)/shard_map/cond/branch_1_fun/while/body/eval_jaxpr/reduce_sum | solution.py:25
  253.2 7.3 %fusion.122 = f32[1024,4,64]{0,2,1:T(8,128)S(1)} fusion(f32[4,1024,1024]{2,1,0:T(8,128)} %get-tuple-element.373, f32[4,1024]{1,0:T(4,128)S(1)} %get-tuple-element.371, bf16[1024,2,4,64]{0,3,2,1:T(8,128)(2,1)S(1)} %dynamic-slice_bitcast_fusion.2, f32[1024,4]{0,1:T(4,128)S(1)} %get-tuple-element.375), kind=kOutput, calls=%fused_computation.27.clone.1 | convolution fusion | flops 545521664 | bytes 18382848 | tf_op jit(solution)/shard_map/cond/branch_1_fun/while/body/eval_jaxpr/rij,jrx->irx/dot_general | solution.py:26
  263.1 9.2 %bitcast_reduce_fusion.2 = (f32[4,1024]{1,0:T(4,128)S(1)}, f32[4,1024,1024]{2,1,0:T(8,128)}) fusion(bf16[1024,4,64]{0,2,1:T(8,128)(2,1)} %get-tuple-element.398, bf16[1024,2,4,64]{0,3,2,1:T(8,128)(2,1)S(1)} %dynamic-slice_bitcast_fusion.2), kind=kOutput, calls=%fused_computation.20.clone.1 | convolution fusion | flops 541061120 | bytes 17842176 | tf_op jit(solution)/shard_map/cond/branch_1_fun/while/body/eval_jaxpr/wux,jux->uwj/dot_general | solution.py:19
  273.0 8.0 %fusion.120 = f32[4,1024]{1,0:T(4,128)S(1)} fusion(f32[4,1024,1024]{2,1,0:T(8,128)} %get-tuple-element.373, f32[4,1024]{1,0:T(4,128)S(1)} %get-tuple-element.371), kind=kLoop, calls=%fused_computation.23.clone.1 | loop fusion | flops 8384512 | bytes 16809984 | tf_op jit(solution)/shard_map/cond/branch_1_fun/while/body/eval_jaxpr/reduce_sum | solution.py:25
  283.0 7.3 %fusion.122 = f32[1024,4,64]{0,2,1:T(8,128)S(1)} fusion(f32[4,1024,1024]{2,1,0:T(8,128)} %get-tuple-element.373, f32[4,1024]{1,0:T(4,128)S(1)} %get-tuple-element.371, bf16[1024,2,4,64]{0,3,2,1:T(8,128)(2,1)S(1)} %dynamic-slice_bitcast_fusion.2, f32[1024,4]{0,1:T(4,128)S(1)} %get-tuple-element.375), kind=kOutput, calls=%fused_computation.27.clone.1 | convolution fusion | flops 545521664 | bytes 18382848 | tf_op jit(solution)/shard_map/cond/branch_1_fun/while/body/eval_jaxpr/rij,jrx->irx/dot_general | solution.py:26
  292.9 9.2 %bitcast_reduce_fusion.2 = (f32[4,1024]{1,0:T(4,128)S(1)}, f32[4,1024,1024]{2,1,0:T(8,128)}) fusion(bf16[1024,4,64]{0,2,1:T(8,128)(2,1)} %get-tuple-element.398, bf16[1024,2,4,64]{0,3,2,1:T(8,128)(2,1)S(1)} %dynamic-slice_bitcast_fusion.2), kind=kOutput, calls=%fused_computation.20.clone.1 | convolution fusion | flops 541061120 | bytes 17842176 | tf_op jit(solution)/shard_map/cond/branch_1_fun/while/body/eval_jaxpr/wux,jux->uwj/dot_general | solution.py:19
  302.8 8.0 %fusion.120 = f32[4,1024]{1,0:T(4,128)S(1)} fusion(f32[4,1024,1024]{2,1,0:T(8,128)} %get-tuple-element.373, f32[4,1024]{1,0:T(4,128)S(1)} %get-tuple-element.371), kind=kLoop, calls=%fused_computation.23.clone.1 | loop fusion | flops 8384512 | bytes 16809984 | tf_op jit(solution)/shard_map/cond/branch_1_fun/while/body/eval_jaxpr/reduce_sum | solution.py:25
  312.8 7.3 %fusion.122 = f32[1024,4,64]{0,2,1:T(8,128)S(1)} fusion(f32[4,1024,1024]{2,1,0:T(8,128)} %get-tuple-element.373, f32[4,1024]{1,0:T(4,128)S(1)} %get-tuple-element.371, bf16[1024,2,4,64]{0,3,2,1:T(8,128)(2,1)S(1)} %dynamic-slice_bitcast_fusion.2, f32[1024,4]{0,1:T(4,128)S(1)} %get-tuple-element.375), kind=kOutput, calls=%fused_computation.27.clone.1 | convolution fusion | flops 545521664 | bytes 18382848 | tf_op jit(solution)/shard_map/cond/branch_1_fun/while/body/eval_jaxpr/rij,jrx->irx/dot_general | solution.py:26
  322.7 9.2 %bitcast_reduce_fusion.2 = (f32[4,1024]{1,0:T(4,128)S(1)}, f32[4,1024,1024]{2,1,0:T(8,128)}) fusion(bf16[1024,4,64]{0,2,1:T(8,128)(2,1)} %get-tuple-element.398, bf16[1024,2,4,64]{0,3,2,1:T(8,128)(2,1)S(1)} %dynamic-slice_bitcast_fusion.2), kind=kOutput, calls=%fused_computation.20.clone.1 | convolution fusion | flops 541061120 | bytes 17842176 | tf_op jit(solution)/shard_map/cond/branch_1_fun/while/body/eval_jaxpr/wux,jux->uwj/dot_general | solution.py:19
  332.6 8.0 %fusion.120 = f32[4,1024]{1,0:T(4,128)S(1)} fusion(f32[4,1024,1024]{2,1,0:T(8,128)} %get-tuple-element.373, f32[4,1024]{1,0:T(4,128)S(1)} %get-tuple-element.371), kind=kLoop, calls=%fused_computation.23.clone.1 | loop fusion | flops 8384512 | bytes 16809984 | tf_op jit(solution)/shard_map/cond/branch_1_fun/while/body/eval_jaxpr/reduce_sum | solution.py:25
  342.6 7.3 %fusion.122 = f32[1024,4,64]{0,2,1:T(8,128)S(1)} fusion(f32[4,1024,1024]{2,1,0:T(8,128)} %get-tuple-element.373, f32[4,1024]{1,0:T(4,128)S(1)} %get-tuple-element.371, bf16[1024,2,4,64]{0,3,2,1:T(8,128)(2,1)S(1)} %dynamic-slice_bitcast_fusion.2, f32[1024,4]{0,1:T(4,128)S(1)} %get-tuple-element.375), kind=kOutput, calls=%fused_computation.27.clone.1 | convolution fusion | flops 545521664 | bytes 18382848 | tf_op jit(solution)/shard_map/cond/branch_1_fun/while/body/eval_jaxpr/rij,jrx->irx/dot_general | solution.py:26
  365.1 42.1 %reduce-scatter.3.cloned.1.call-done = f32[256,1024]{1,0:T(8,128)} async-done(((f32[1024,1024]{1,0:T(8,128)}), f32[256,1024]{1,0:T(8,128)}) %reduce-scatter.3.cloned.1.call-update) | async-done | bytes 1048592 | tf_op jit(solution)/shard_map/reduce_scatter | solution.py:146
  412.8 22.5 %all-gather.7.cloned.1.call-done = bf16[1024,1024]{1,0:T(8,128)(2,1)} async-done(((bf16[256,1024]{1,0:T(8,128)(2,1)}), bf16[1024,1024]{1,0:T(8,128)(2,1)}) %all-gather.7.cloned.1.call-update) | async-done | bytes 2097168 | tf_op jit(solution)/shard_map/all_gather | solution.py:159
  435.3 15.8 %fusion.40 = f32[1024,1024]{1,0:T(8,128)} fusion(bf16[1024,1024]{1,0:T(8,128)(2,1)S(1)} %copy-done, f32[1024]{0:T(1024)S(1)} %copy-done.16, bf16[1024,1024]{1,0:T(8,128)(2,1)} %all-gather.7.cloned.1.call-done, bf16[1024,1024]{1,0:T(8,128)(2,1)} %param.31), kind=kOutput, calls=%fused_computation.65 | convolution fusion | flops 4364173312 | bytes 10489856 | tf_op jit(solution)/shard_map/dot_general | solution.py:168
  457.1 38.8 %reduce-scatter.5.cloned.1.call-done = f32[256,1024]{1,0:T(8,128)} async-done(((f32[1024,1024]{1,0:T(8,128)}), f32[256,1024]{1,0:T(8,128)}) %reduce-scatter.5.cloned.1.call-update) | async-done | bytes 1048592 | tf_op jit(solution)/shard_map/reduce_scatter | solution.py:167
  (137 shorter events, 76.6 us)
Async XLA Ops:
  7.2 428.1 %copy-start = (bf16[1024,1024]{1,0:T(8,128)(2,1)S(1)}, bf16[1024,1024]{1,0:T(8,128)(2,1)}, u32[]{:S(2)}) copy-start(bf16[1024,1024]{1,0:T(8,128)(2,1)} %param.33) | copy-start | bytes 6291460
  7.2 5.8 %copy-start.13 = (s32[3]{0:T(128)S(1)}, s32[3]{0:T(128)}, u32[]{:S(2)}) copy-start(s32[3]{0:T(128)} %param.26) | copy-start | bytes 40
  7.2 27.7 %all-gather.9.cloned.1.call-start = ((), (), s32[]{:S(2)}) async-start(), calls=%async_computation.6 | async-start | bytes 2621440 | tf_op jit(solution)/shard_map/all_gather | solution.py:91
  7.9 205.1 %all-gather.5.cloned.1.call-start = ((), (), s32[]{:S(2)}) async-start(), calls=%async_computation.2 | async-start | bytes 14155776 | tf_op jit(solution)/shard_map/all_gather | solution.py:135
  12.9 394.4 %reduce-scatter.3.cloned.1.call-start = ((), (), s32[]{:S(2)}) async-start(), calls=%async_computation.3 | async-start | bytes 5242880 | tf_op jit(solution)/shard_map/reduce_scatter | solution.py:146
  14.8 20.1 %copy-start.15 = (f32[3,256]{1,0:T(4,128)S(1)}, f32[3,256]{1,0:T(4,128)}, u32[]{:S(2)}) copy-start(f32[3,256]{1,0:T(4,128)} %param.28) | copy-start | bytes 9220
  14.8 20.1 %copy-start.17 = (f32[3]{0:T(128)S(1)}, f32[3]{0:T(128)}, u32[]{:S(2)}) copy-start(f32[3]{0:T(128)} %constant.147.clone) | copy-start | bytes 40
  34.9 5.0 copy-start.7
  38.9 2.8 copy-start.6
  41.6 171.5 %copy-start.14 = (pred[3]{0:T(512)(128)(4,1)S(1)}, pred[3]{0:T(512)(128)(4,1)}, u32[]{:S(2)}) copy-start(pred[3]{0:T(512)(128)(4,1)} %get-tuple-element.242) | copy-start | bytes 13
  49.6 7.3 %copy-start.1 = (f32[4,512,2560]{2,1,0:T(8,128)}, f32[4,512,2560]{2,1,0:T(8,128)S(1)}, u32[]{:S(2)}) copy-start(f32[4,512,2560]{2,1,0:T(8,128)S(1)} %get-tuple-element.361) | copy-start | bytes 62914564 | tf_op jit(solution)/shard_map/while
  77.1 7.3 %copy-start.1 = (f32[4,512,2560]{2,1,0:T(8,128)}, f32[4,512,2560]{2,1,0:T(8,128)S(1)}, u32[]{:S(2)}) copy-start(f32[4,512,2560]{2,1,0:T(8,128)S(1)} %get-tuple-element.361) | copy-start | bytes 62914564 | tf_op jit(solution)/shard_map/while
  253.2 7.3 %copy-start.2 = (f32[1024,256]{0,1:T(8,128)S(1)}, f32[1024,256]{0,1:T(8,128)}, u32[]{:S(2)}) copy-start(f32[1024,256]{0,1:T(8,128)} %get-tuple-element.388) | copy-start | bytes 3145732 | tf_op jit(solution)/shard_map/cond/branch_1_fun/while
  260.8 1.0 copy-start.3
  283.0 7.3 %copy-start.2 = (f32[1024,256]{0,1:T(8,128)S(1)}, f32[1024,256]{0,1:T(8,128)}, u32[]{:S(2)}) copy-start(f32[1024,256]{0,1:T(8,128)} %get-tuple-element.388) | copy-start | bytes 3145732 | tf_op jit(solution)/shard_map/cond/branch_1_fun/while
  290.6 1.0 copy-start.3
  312.8 7.3 %copy-start.2 = (f32[1024,256]{0,1:T(8,128)S(1)}, f32[1024,256]{0,1:T(8,128)}, u32[]{:S(2)}) copy-start(f32[1024,256]{0,1:T(8,128)} %get-tuple-element.388) | copy-start | bytes 3145732 | tf_op jit(solution)/shard_map/cond/branch_1_fun/while
  320.4 1.0 copy-start.3
  342.6 7.3 %copy-start.2 = (f32[1024,256]{0,1:T(8,128)S(1)}, f32[1024,256]{0,1:T(8,128)}, u32[]{:S(2)}) copy-start(f32[1024,256]{0,1:T(8,128)} %get-tuple-element.388) | copy-start | bytes 3145732 | tf_op jit(solution)/shard_map/cond/branch_1_fun/while
  350.2 1.0 copy-start.3
  358.8 2.9 copy-start.8
  364.4 0.7 copy-start.11
  364.4 0.7 copy-start.12
  364.4 42.9 %copy-start.5 = (bf16[1,256,1024]{2,1,0:T(8,128)(2,1)S(1)}, bf16[1,256,1024]{2,1,0:T(8,128)(2,1)}, u32[]{:S(2)}) copy-start(bf16[1,256,1024]{2,1,0:T(8,128)(2,1)} %param.22) | copy-start | bytes 1572868
  364.4 42.9 %copy-start.9 = (f32[1024]{0:T(1024)S(1)}, f32[1024]{0:T(1024)}, u32[]{:S(2)}) copy-start(f32[1024]{0:T(1024)} %param.30) | copy-start | bytes 12292
  364.4 70.9 %copy-start.16 = (f32[1024]{0:T(1024)S(1)}, f32[1024]{0:T(1024)}, u32[]{:S(2)}) copy-start(f32[1024]{0:T(1024)} %param.32) | copy-start | bytes 12292
  364.4 70.9 %all-gather.7.cloned.1.call-start = ((), (), s32[]{:S(2)}) async-start(), calls=%async_computation.4 | async-start | bytes 2621440 | tf_op jit(solution)/shard_map/all_gather | solution.py:159
  412.5 83.3 %reduce-scatter.5.cloned.1.call-start = ((), (), s32[]{:S(2)}) async-start(), calls=%async_computation.5 | async-start | bytes 5242880 | tf_op jit(solution)/shard_map/reduce_scatter | solution.py:167
  451.1 44.8 %copy-start.4 = (bf16[256,1024]{1,0:T(8,128)(2,1)S(1)}, bf16[256,1024]{1,0:T(8,128)(2,1)}, u32[]{:S(2)}) copy-start(bf16[256,1024]{1,0:T(8,128)(2,1)} %add_convert_fusion.1) | copy-start | bytes 1572868
  451.1 44.8 %copy-start.10 = (f32[1024]{0:T(1024)S(1)}, f32[1024]{0:T(1024)}, u32[]{:S(2)}) copy-start(f32[1024]{0:T(1024)} %param.34) | copy-start | bytes 12292
Sparse Core Ops, SparseCore 0:
  9.6 25.2 all-gather.8
  36.9 176.0 all-gather.4
  364.5 42.6 reduce-scatter.2
  412.7 22.5 all-gather.6
  451.2 44.5 reduce-scatter.4
where the time goes:
time: 510 us; the launch traced here: 508 us
  waiting for transfers between devices  226 us (44%)
  matrix products  119 us (23%)
  other arithmetic  75.4 us (15%)
  local copies, waits for them, and re-layouts  68.7 us (13%)
  between operations  14.6 us (3%)
    all_gather x1, waiting for transfers between devices, body(): stripes = lax.all_gather(long_cache, 'req', axis=1, tiled=True)  116 us
    dot_general x6, matrix products, partial_attend(): jnp.einsum('rij,jrx->irx', softmax_weights.astype(jnp.bfloat16), value_ma...  50.2 us
    dot_general x6, matrix products, partial_attend(): jnp.einsum('wux,jux->uwj', query_matrix, key_matrix, preferred_element_ty...  46.5 us
    reduce_sum x6, other arithmetic, partial_attend(): row_total = jnp.sum(softmax_weights, axis=2)  46.4 us
    reduce_scatter x1, waiting for transfers between devices, body(): lax.psum_scatter(jnp.dot(context, w_out, preferred_element_type=jnp.float...  42.1 us
    reduce_scatter x1, waiting for transfers between devices, body(): lax.psum_scatter(jnp.dot(units, w_down, preferred_element_type=jnp.float3...  38.8 us
    all_gather x1, waiting for transfers between devices, body(): lax.all_gather(normed, 'tp', axis=0, tiled=True)  22.5 us
    dot_general x1, matrix products, body(): jnp.dot(units, w_down, preferred_element_type=jnp.float32)  15.8 us
  transfers between devices with their start and end apart: 5, of which 5 were waited for; matrix products, arithmetic and copies ran while one was open for 17% of the time, Pallas kernels for 0%

commit v1 on v0

v1 whole, which is shorter than its diff:
```python
import functools

import jax
import jax.numpy as jnp
from jax import lax
from jax.experimental import pallas as pl
from jax.experimental.pallas import tpu as pltpu
from jax.sharding import PartitionSpec as P

HEAD_DIM = 64
masked_score = -1e30
TQ = 512
TK = 512


def layer_norm(rows_in, gain, shift):
    center = rows_in - jnp.mean(rows_in, axis=-1, keepdims=True)
    spread = jnp.mean(center * center, axis=-1, keepdims=True)
    return center * lax.rsqrt(spread + 1e-05) * gain + shift


def _attend_block(q_ref, k_ref, v_ref, m_sc, l_sc, acc_sc, valid):
    width = q_ref.shape[1]
    col = lax.broadcasted_iota(jnp.int32, (q_ref.shape[0], 128), 1)
    low = col < HEAD_DIM
    for pair in range(width // 128):
        cols = slice(pair * 128, (pair + 1) * 128)
        q2 = q_ref[:, cols]
        k2 = k_ref[:, cols]
        v2 = v_ref[:, cols]
        alphas = []
        pvs = []
        for half in range(2):
            h = pair * 2 + half
            qh = jnp.where(low if half == 0 else jnp.logical_not(low), q2, jnp.zeros_like(q2))
            s = lax.dot_general(
                qh, k2, (((1,), (1,)), ((), ())), preferred_element_type=jnp.float32
            )
            if valid is not None:
                s = jnp.where(valid, s, masked_score)
            m_prev = m_sc[h]
            m_new = jnp.maximum(m_prev, jnp.max(s, axis=1, keepdims=True))
            alpha = jnp.exp(m_prev - m_new)
            p = jnp.exp(s - m_new[:, 0:1])
            l_sc[h] = alpha * l_sc[h] + jnp.sum(p, axis=1, keepdims=True)
            m_sc[h] = m_new
            pvs.append(jnp.dot(p.astype(jnp.bfloat16), v2, preferred_element_type=jnp.float32))
            alphas.append(alpha)
        alpha2 = jnp.where(low, alphas[0], alphas[1])
        acc_sc[:, cols] = alpha2 * acc_sc[:, cols] + jnp.where(low, pvs[0], pvs[1])


def _local_kernel(sref, q_ref, k_ref, v_ref, m_out, l_out, acc_out, m_sc, l_sc, acc_sc, *, n_short, nk):
    i = pl.program_id(0)
    j = pl.program_id(1)
    short_len = sref[0]

    @pl.when(j == 0)
    def _():
        m_sc[...] = jnp.full(m_sc.shape, masked_score, jnp.float32)
        l_sc[...] = jnp.zeros(l_sc.shape, jnp.float32)
        acc_sc[...] = jnp.zeros(acc_sc.shape, jnp.float32)

    is_short = j < n_short
    c = j - n_short
    first_row = i * TQ
    full = jnp.where(is_short, (j + 1) * TK <= short_len, c * TK + TK - 1 <= first_row)
    some = jnp.where(is_short, j * TK < short_len, c * TK <= first_row + TQ - 1)

    @pl.when(full)
    def _():
        _attend_block(q_ref, k_ref, v_ref, m_sc, l_sc, acc_sc, None)

    @pl.when(jnp.logical_and(some, jnp.logical_not(full)))
    def _():
        rows = lax.broadcasted_iota(jnp.int32, (TQ, TK), 0) + first_row
        keys = lax.broadcasted_iota(jnp.int32, (TQ, TK), 1)
        bound = jnp.where(is_short, short_len - j * TK, rows - c * TK + 1)
        valid = keys < bound
        _attend_block(q_ref, k_ref, v_ref, m_sc, l_sc, acc_sc, valid)

    @pl.when(j == nk - 1)
    def _():
        m_out[...] = m_sc[...]
        l_out[...] = l_sc[...]
        acc_out[...] = acc_sc[...]


def _long_kernel(sref, q_ref, k_ref, v_ref, m_in, l_in, acc_in, o_ref, m_sc, l_sc, acc_sc, *, nk):
    j = pl.program_id(1)

    @pl.when(j == 0)
    def _():
        m_sc[...] = m_in[...]
        l_sc[...] = l_in[...]
        acc_sc[...] = acc_in[...]

    @pl.when(sref[1] > 0)
    def _():
        _attend_block(q_ref, k_ref, v_ref, m_sc, l_sc, acc_sc, None)

    @pl.when(j == nk - 1)
    def _():
        width = o_ref.shape[1]
        col = lax.broadcasted_iota(jnp.int32, (TQ, 128), 1)
        for pair in range(width // 128):
            cols = slice(pair * 128, (pair + 1) * 128)
            total = jnp.where(col < HEAD_DIM, l_sc[2 * pair], l_sc[2 * pair + 1])
            o_ref[:, cols] = (acc_sc[:, cols] / total).astype(o_ref.dtype)


def local_attention(scalars, q, kv, n_short):
    span, width = q.shape
    heads = width // HEAD_DIM
    nq = span // TQ
    nk = kv.shape[0] // TK

    def kv_block(i, j, s):
        last_short = (s[0] - 1) // TK
        last_new = (i * TQ + TQ - 1) // TK
        return jnp.where(
            j < n_short, jnp.minimum(j, last_short), n_short + jnp.minimum(j - n_short, last_new)
        )

    stat_spec = pl.BlockSpec((heads, TQ, 128), lambda i, j, s: (0, i, 0))
    grid_spec = pltpu.PrefetchScalarGridSpec(
        num_scalar_prefetch=1,
        grid=(nq, nk),
        in_specs=[
            pl.BlockSpec((TQ, width), lambda i, j, s: (i, 0)),
            pl.BlockSpec((TK, width), lambda i, j, s: (kv_block(i, j, s), 0)),
            pl.BlockSpec((TK, width), lambda i, j, s: (kv_block(i, j, s), 1)),
        ],
        out_specs=[stat_spec, stat_spec, pl.BlockSpec((TQ, width), lambda i, j, s: (i, 0))],
        scratch_shapes=[
            pltpu.VMEM((heads, TQ, 128), jnp.float32),
            pltpu.VMEM((heads, TQ, 128), jnp.float32),
            pltpu.VMEM((TQ, width), jnp.float32),
        ],
    )
    return pl.pallas_call(
        functools.partial(_local_kernel, n_short=n_short, nk=nk),
        grid_spec=grid_spec,
        out_shape=[
            jax.ShapeDtypeStruct((heads, span, 128), jnp.float32),
            jax.ShapeDtypeStruct((heads, span, 128), jnp.float32),
            jax.ShapeDtypeStruct((span, width), jnp.float32),
        ],
        compiler_params=pltpu.CompilerParams(dimension_semantics=("arbitrary", "arbitrary")),
    )(scalars, q, kv, kv)


def long_attention(scalars, q, kv, m, l, acc):
    span, width = q.shape
    heads = width // HEAD_DIM
    nq = span // TQ
    nk = kv.shape[0] // TK
    stat_spec = pl.BlockSpec((heads, TQ, 128), lambda i, j, s: (0, i, 0))
    row_spec = pl.BlockSpec((TQ, width), lambda i, j, s: (i, 0))
    grid_spec = pltpu.PrefetchScalarGridSpec(
        num_scalar_prefetch=1,
        grid=(nq, nk),
        in_specs=[
            row_spec,
            pl.BlockSpec((TK, width), lambda i, j, s: (j * s[1], 0)),
            pl.BlockSpec((TK, width), lambda i, j, s: (j * s[1], 1)),
            stat_spec,
            stat_spec,
            row_spec,
        ],
        out_specs=row_spec,
        scratch_shapes=[
            pltpu.VMEM((heads, TQ, 128), jnp.float32),
            pltpu.VMEM((heads, TQ, 128), jnp.float32),
            pltpu.VMEM((TQ, width), jnp.float32),
        ],
    )
    return pl.pallas_call(
        functools.partial(_long_kernel, nk=nk),
        grid_spec=grid_spec,
        out_shape=jax.ShapeDtypeStruct((span, width), jnp.bfloat16),
        compiler_params=pltpu.CompilerParams(dimension_semantics=("arbitrary", "arbitrary")),
    )(scalars, q, kv, kv, m, l, acc)


def solution(mesh):
    n_req = mesh.shape["req"]

    def body(
        hidden_in,
        short_cache,
        long_cache,
        short_len,
        long_owner,
        w_qkv,
        b_qkv,
        w_out,
        b_out,
        w_in,
        b_in,
        w_down,
        b_down,
        norm_gain,
        norm_offset,
    ):
        n_long = long_cache.shape[0]
        long_ids = jnp.arange(n_long, dtype=jnp.int32)

        def which_long(request):
            owned = long_owner == request
            return jnp.sum(jnp.where(owned, long_ids, 0)), jnp.any(owned)

        me = lax.axis_index("req")
        my_long, has_long = which_long(me)
        stripes = [lax.dynamic_index_in_dim(long_cache, my_long, 0, keepdims=False)]
        for shift in range(1, n_req):
            dest_long, unused = which_long((me + shift) % n_req)
            chunk = lax.dynamic_index_in_dim(long_cache, dest_long, 0, keepdims=False)
            stripes.append(
                lax.ppermute(chunk, "req", [(k, (k + shift) % n_req) for k in range(n_req)])
            )
        long_kv = jnp.concatenate(stripes, axis=0)
        long_kv = long_kv.reshape(long_kv.shape[0], -1)

        w_out_full = lax.all_gather(w_out, "tp", axis=0, tiled=True)

        local_rows = hidden_in[0]
        factors = jnp.array([0.125, 1.0, 1.0], jnp.float32)[None, :, None]
        mixed = jnp.einsum(
            "nd,cdk->nck",
            lax.all_gather(local_rows, "tp", axis=0, tiled=True),
            w_qkv,
            preferred_element_type=jnp.float32,
        )
        projected = ((mixed + b_qkv[None]) * factors).astype(jnp.bfloat16)
        span_len = projected.shape[0]
        queries = projected[:, 0]
        new_kv = projected[None, :, 1:3]
        short_rows = short_cache[0]
        cache_len = short_rows.shape[0]
        local_kv = jnp.concatenate(
            [short_rows.reshape(cache_len, -1), projected[:, 1:3].reshape(span_len, -1)], axis=0
        )
        scalars = jnp.stack([short_len[0], has_long.astype(jnp.int32)])
        m, l, acc = local_attention(scalars, queries, local_kv, cache_len // TK)
        context = long_attention(scalars, queries, long_kv, m, l, acc)

        context_rows = lax.all_to_all(context, "tp", 0, 1, tiled=True)
        attended = jnp.dot(context_rows, w_out_full, preferred_element_type=jnp.float32) + b_out
        normed = layer_norm(
            local_rows.astype(jnp.float32) + attended, norm_gain[0], norm_offset[0]
        ).astype(jnp.bfloat16)
        units = jax.nn.gelu(
            jnp.dot(
                lax.all_gather(normed, "tp", axis=0, tiled=True),
                w_in,
                preferred_element_type=jnp.float32,
            )
            + b_in,
            approximate=False,
        ).astype(jnp.bfloat16)
        mixed = (
            lax.psum_scatter(
                jnp.dot(units, w_down, preferred_element_type=jnp.float32),
                "tp",
                scatter_dimension=0,
                tiled=True,
            )
            + b_down
        )
        hidden_out = layer_norm(
            normed.astype(jnp.float32) + mixed, norm_gain[1], norm_offset[1]
        ).astype(jnp.bfloat16)
        return (hidden_out[None], new_kv)

    return jax.shard_map(
        body,
        mesh=mesh,
        in_specs=(
            P("req", "tp", None),
            P("req", None, None, "tp"),
            P(None, "req", None, "tp"),
            P("req"),
            P(),
            P(None, None, "tp"),
            P(None, "tp"),
            P("tp", None),
            P(),
            P(None, "tp"),
            P("tp"),
            P("tp", None),
            P(),
            P(),
            P(),
        ),
        out_specs=(P("req", "tp", None), P("req", None, None, "tp")),
        check_vma=False,
    )
```

time: 510 us -> 333 us (0.65)
  matrix products: 119 us -> 22.4 us
  waiting for transfers between devices: 226 us -> 137 us
  Pallas kernels: 0 us -> 66.9 us
  other arithmetic: 75.4 us -> 12.2 us
  local copies, waits for them, and re-layouts: 68.7 us -> 37 us
  starting transfers between devices: 0.42 us -> 27.3 us
  between operations: 14.6 us -> 30.5 us
    all_gather x1, waiting for transfers between devices: 116 us -> 0.02 us  [body(): w_out_full = lax.all_gather(w_out, 'tp', axis=0, tiled=True)]
    dot_general x13 -> x1, matrix products: 99.3 us -> 2.65 us  [body(): jnp.dot(context_rows, w_out_full, preferred_element_type=jnp.float32)]
    pallas_call x0 -> x2, Pallas kernels: none -> 66.9 us  [the longest x1 42.3 us: long_attention(): pl.pallas_call(functools.partial(_long_kernel, nk=nk), grid_spec=grid_spe...]
    reduce_sum x7 -> x1, other arithmetic: 47 us -> 1.44 us  [which_long(): return (jnp.sum(jnp.where(owned, long_ids, 0)), jnp.any(owned))]
    reduce_scatter x1 -> x0, waiting for transfers between devices: 42.1 us -> none  [body(): lax.psum_scatter(jnp.dot(context, w_out, preferred_element_type=jnp.float...]
    ppermute x0 -> x7, waiting for transfers between devices: none -> 35.2 us  [body(): lax.ppermute(chunk, 'req', [(k, (k + shift) % n_req) for k in range(n_req)])]
    all_gather x1, waiting for transfers between devices: 22.5 us -> 51.1 us  [body(): lax.all_gather(normed, 'tp', axis=0, tiled=True)]
    ppermute x0 -> x7, starting transfers between devices: none -> 23.3 us  [body(): lax.ppermute(chunk, 'req', [(k, (k + shift) % n_req) for k in range(n_req)])]
  transfers between devices with their start and end apart: 5 -> 12, of which waited for: 5 -> 6; matrix products, arithmetic and copies ran while one was open for 17% -> 13% of each run, Pallas kernels for 0% -> 20%
where the time goes in v1:
time: 333 us
  waiting for transfers between devices  137 us (41%)
  Pallas kernels  66.9 us (20%)
  local copies, waits for them, and re-layouts  37 us (11%)
  between operations  30.5 us (9%)
  starting transfers between devices  27.3 us (8%)
  matrix products  22.4 us (7%)
  other arithmetic  12.2 us (4%)
    all_gather x1, waiting for transfers between devices, body(): lax.all_gather(normed, 'tp', axis=0, tiled=True)  51.1 us
    pallas_call x1, Pallas kernels, long_attention(): pl.pallas_call(functools.partial(_long_kernel, nk=nk), grid_spec=grid_spe...  42.3 us
    reduce_scatter x1, waiting for transfers between devices, body(): lax.psum_scatter(jnp.dot(units, w_down, preferred_element_type=jnp.float3...  41.5 us
    ppermute x7, waiting for transfers between devices, body(): lax.ppermute(chunk, 'req', [(k, (k + shift) % n_req) for k in range(n_req)])  35.2 us
    pallas_call x1, Pallas kernels, local_attention(): pl.pallas_call(functools.partial(_local_kernel, n_short=n_short, nk=nk),...  24.6 us
    ppermute x7, starting transfers between devices, body(): lax.ppermute(chunk, 'req', [(k, (k + shift) % n_req) for k in range(n_req)])  23.3 us
    unnamed x41, local copies, waits for them, and re-layouts  22.1 us
    dot_general x1, matrix products, body(): jnp.dot(units, w_down, preferred_element_type=jnp.float32)  15.8 us
  transfers between devices with their start and end apart: 12, of which 6 were waited for; matrix products, arithmetic and copies ran while one was open for 13% of the time, Pallas kernels for 20%

profile of v1, /device:TPU:0, one launch (start us, length us, event | category | flops | bytes accessed | tf_op | source)
XLA Modules:
  0.0 333.3 jit_solution(5583530714567940449)
XLA Ops:
  8.0 1.4 fusion.28
  24.6 6.3 %dynamic-slice_bitcast_fusion = (bf16[512,2,256]{2,1,0:T(2,128)(2,1)}, bf16[512,2,256]{2,1,0:T(2,128)(2,1)}, bf16[512,2,256]{2,1,0:T(2,128)(2,1)}, bf16[512,2,25...) fusion(bf16[3,512,2,256]{3,2,1,0:T(2,128)(2,1)} %param.18, ...), kind=kLoop, calls=%fused_computation.34 | loop fusion | bytes 8388640 | tf_op jit(solution)/shard_map/jit(dynamic_index_in_dim)/squeeze | solution.py:218
  30.9 2.9 collective-permute-start
  33.8 1.6 collective-permute-start.1
  35.4 2.6 collective-permute-start.2
  38.0 1.3 collective-permute-start.3
  39.3 2.6 collective-permute-start.4
  41.9 8.1 %collective-permute-done = bf16[512,2,256]{2,1,0:T(2,128)(2,1)} collective-permute-done((bf16[512,2,256]{2,1,0:T(2,128)(2,1)S(1)}, bf16[512,2,256]{2,1,0:T(2,128)(2,1)}, u32[]{:S(2)}, u32[]{:S(2)}) %collective-permute-start) | collective-permute-done | bytes 524320 | tf_op jit(solution)/shard_map/ppermute | solution.py:220
  50.0 1.8 collective-permute-start.5
  51.8 10.5 %collective-permute-start.6 = (bf16[512,2,256]{2,1,0:T(2,128)(2,1)}, bf16[512,2,256]{2,1,0:T(2,128)(2,1)}, u32[]{:S(2)}, u32[]{:S(2)}) collective-permute-start(bf16[512,2,256]{2,1,0:T(2,128)(2,1)} %get-tuple-element.22), channel_id=1, source_target_pairs={{0,28},{4,0},{8,4},{12,8},{16,12},{20,16},{24,20},{28,24},{1,29},{... | collective-permute-start | bytes 1572872 | tf_op jit(solution)/shard_map/ppermute | solution.py:220
  64.3 2.9 copy.37
  71.0 23.0 %collective-permute-done.2 = bf16[512,2,256]{2,1,0:T(2,128)(2,1)} collective-permute-done((bf16[512,2,256]{2,1,0:T(2,128)(2,1)}, bf16[512,2,256]{2,1,0:T(2,128)(2,1)}, u32[]{:S(2)}, u32[]{:S(2)}) %collective-permute-start.2) | collective-permute-done | bytes 524320 | tf_op jit(solution)/shard_map/ppermute | solution.py:220
  98.6 4.1 %collective-permute-done.6 = bf16[512,2,256]{2,1,0:T(2,128)(2,1)} collective-permute-done((bf16[512,2,256]{2,1,0:T(2,128)(2,1)}, bf16[512,2,256]{2,1,0:T(2,128)(2,1)}, u32[]{:S(2)}, u32[]{:S(2)}) %collective-permute-start.6) | collective-permute-done | bytes 524320 | tf_op jit(solution)/shard_map/ppermute | solution.py:220
  109.7 4.0 %multiply_convert_fusion = bf16[1024,3,256]{2,0,1:T(8,128)(2,1)S(1)} fusion(f32[3]{0:T(128)S(1)} %copy-done.11, f32[3,256]{1,0:T(4,128)S(1)} %copy-done.9, bf16[3,1024,256]{2,1,0:T(8,128)(2,1)} %param.21, bf16[1,1024,1024]{2,1,0:T(8,128)(2,1)} %all-gather.9.cloned.1.call-done), kind=kOutput, calls=%fused_computation.19 | convolution fusion | flops 1612972032 | bytes 5245964 | tf_op jit(solution)/shard_map/nd,cdk->nck/dot_general | solution.py:229
  113.7 1.2 copy-done.3
  116.0 1.3 copy.23
  117.3 1.5 copy.24
  118.8 1.9 slice_bitcast_fusion.q_ref
  120.7 3.1 pad_maximum_fusion.k_ref.v_ref
  123.8 24.6 %shard_map.167 = (f32[4,1024,128]{2,1,0:T(8,128)}, f32[4,1024,128]{2,1,0:T(8,128)}, f32[1024,256]{1,0:T(8,128)}) custom-call(s32[2]{0:T(128)} %pad_add_fusion.sref, bf16[1024,256]{1,0:T(8,128)(2,1)} %slice_bitcast_fusion.q_ref, bf16[2560,512]{1,0:T(8,128)(2,1)} %pad_maximum_fusion.k_ref.v_ref, bf16[2560,512]{1,0:T(8,128)(2,1)} %pad_maximum_fusion.k_ref.v_ref), custom_call_target="tpu_custom_call" | custom-call | tf_op jit(solution)/shard_map/pallas_call | solution.py:141
  148.4 42.3 %shard_map.168 = bf16[1024,256]{1,0:T(8,128)(2,1)} custom-call(s32[2]{0:T(128)} %pad_add_fusion.sref, bf16[1024,256]{1,0:T(8,128)(2,1)} %slice_bitcast_fusion.q_ref, bf16[4096,512]{1,0:T(8,128)(2,1)} %constant_dynamic-update-slice_fusion.k_ref.v_ref, bf16[4096,512]{1,0:T(8,128)(2,1)} %constant_dynamic-update-slice_fusion.k_ref.v_ref, ...), custom_call_target="tpu_custom_call" | custom-call | tf_op jit(solution)/shard_map/pallas_call | solution.py:178
  190.8 2.0 copy.25
  192.8 3.6 %all-to-all-start = ((bf16[4,256,256]{1,2,0:T(8,128)(2,1)}), bf16[4,256,256]{1,2,0:T(8,128)(2,1)S(1)}, u32[]{:S(2)}, u32[]{:S(2)}) async-start(bf16[4,256,256]{1,2,0:T(8,128)(2,1)} %copy.25), calls=%async_computation | async-start | bytes 1048576 | tf_op jit(solution)/shard_map/all_to_all | solution.py:248
  196.8 8.4 %all-to-all-done = bf16[4,256,256]{1,2,0:T(8,128)(2,1)S(1)} async-done(((bf16[4,256,256]{1,2,0:T(8,128)(2,1)}), bf16[4,256,256]{1,2,0:T(8,128)(2,1)S(1)}, u32[]{:S(2)}, u32[]{:S(2)}) %all-to-all-start) | async-done | bytes 524320 | tf_op jit(solution)/shard_map/all_to_all | solution.py:248
  206.0 2.6 fusion.61
  210.0 51.1 %all-gather.7.cloned.1.call-done = bf16[1024,1024]{1,0:T(8,128)(2,1)} async-done(((bf16[256,1024]{1,0:T(8,128)(2,1)}), bf16[1024,1024]{1,0:T(8,128)(2,1)}) %all-gather.7.cloned.1.call-update) | async-done | bytes 2097168 | tf_op jit(solution)/shard_map/all_gather | solution.py:255
  261.2 15.8 %fusion.12 = f32[1024,1024]{1,0:T(8,128)} fusion(bf16[1024,1024]{1,0:T(8,128)(2,1)S(1)} %copy-done, f32[1024]{0:T(1024)S(1)} %copy-done.10, bf16[1024,1024]{1,0:T(8,128)(2,1)} %all-gather.7.cloned.1.call-done, bf16[1024,1024]{1,0:T(8,128)(2,1)} %param.25), kind=kOutput, calls=%fused_computation.23 | convolution fusion | flops 4364173312 | bytes 10489856 | tf_op jit(solution)/shard_map/dot_general | solution.py:264
  277.0 3.3 copy.26
  280.3 41.5 %reduce-scatter.2.cloned.1.call-done = f32[256,1024]{1,0:T(8,128)} async-done(((f32[1024,1024]{1,0:T(8,128)}), f32[256,1024]{1,0:T(8,128)}) %reduce-scatter.2.cloned.1.call-update) | async-done | bytes 1048592 | tf_op jit(solution)/shard_map/reduce_scatter | solution.py:263
  321.8 1.7 fusion.20
  323.5 1.7 multiply_reduce_fusion
  325.2 1.6 fusion.19
  (64 shorter events, 20.5 us)
Async XLA Ops:
  7.2 254.0 %copy-start = (bf16[1024,1024]{1,0:T(8,128)(2,1)S(1)}, bf16[1024,1024]{1,0:T(8,128)(2,1)}, u32[]{:S(2)}) copy-start(bf16[1024,1024]{1,0:T(8,128)(2,1)} %param.27) | copy-start | bytes 6291460
  7.2 102.6 %all-gather.9.cloned.1.call-start = ((), (), s32[]{:S(2)}) async-start(), calls=%async_computation.5 | async-start | bytes 2621440 | tf_op jit(solution)/shard_map/all_gather | solution.py:231
  7.9 188.8 %all-gather.5.cloned.1.call-start = ((), (), s32[]{:S(2)}) async-start(), calls=%async_computation.2 | async-start | bytes 2621440 | tf_op jit(solution)/shard_map/all_gather | solution.py:225
  24.6 37.8 %copy-start.8 = (s32[3]{0:T(128)S(1)}, s32[3]{0:T(128)}, u32[]{:S(2)}) copy-start(s32[3]{0:T(128)} %param.20) | copy-start | bytes 40
  30.9 19.1 %collective-permute-start = (bf16[512,2,256]{2,1,0:T(2,128)(2,1)S(1)}, bf16[512,2,256]{2,1,0:T(2,128)(2,1)}, u32[]{:S(2)}, u32[]{:S(2)}) collective-permute-start(bf16[512,2,256]{2,1,0:T(2,128)(2,1)S(1)} %get-tuple-element.27), channel_id=1, source_target_pairs={{0,4},{4,8},{8,12},{12,16},{16,20},{20,24},{24,28},{28,0},{1,5},{5... | collective-permute-start | bytes 1572872 | tf_op jit(solution)/shard_map/ppermute | solution.py:220
  33.8 18.0 %collective-permute-start.1 = (bf16[512,2,256]{2,1,0:T(2,128)(2,1)S(1)}, bf16[512,2,256]{2,1,0:T(2,128)(2,1)}, u32[]{:S(2)}, u32[]{:S(2)}) collective-permute-start(bf16[512,2,256]{2,1,0:T(2,128)(2,1)S(1)} %get-tuple-element.26), channel_id=1, source_target_pairs={{0,8},{4,12},{8,16},{12,20},{16,24},{20,28},{24,0},{28,4},{1,9},{5... | collective-permute-start | bytes 1572872 | tf_op jit(solution)/shard_map/ppermute | solution.py:220
  35.4 58.6 %collective-permute-start.2 = (bf16[512,2,256]{2,1,0:T(2,128)(2,1)}, bf16[512,2,256]{2,1,0:T(2,128)(2,1)}, u32[]{:S(2)}, u32[]{:S(2)}) collective-permute-start(bf16[512,2,256]{2,1,0:T(2,128)(2,1)} %get-tuple-element.25), channel_id=1, source_target_pairs={{0,12},{4,16},{8,20},{12,24},{16,28},{20,0},{24,4},{28,8},{1,13},{... | collective-permute-start | bytes 1572872 | tf_op jit(solution)/shard_map/ppermute | solution.py:220
  38.0 57.1 %collective-permute-start.3 = (bf16[512,2,256]{2,1,0:T(2,128)(2,1)}, bf16[512,2,256]{2,1,0:T(2,128)(2,1)}, u32[]{:S(2)}, u32[]{:S(2)}) collective-permute-start(bf16[512,2,256]{2,1,0:T(2,128)(2,1)} %get-tuple-element.24), channel_id=1, source_target_pairs={{0,16},{4,20},{8,24},{12,28},{16,0},{20,4},{24,8},{28,12},{1,17},{... | collective-permute-start | bytes 1572872 | tf_op jit(solution)/shard_map/ppermute | solution.py:220
  39.3 57.0 %collective-permute-start.4 = (bf16[512,2,256]{2,1,0:T(2,128)(2,1)}, bf16[512,2,256]{2,1,0:T(2,128)(2,1)}, u32[]{:S(2)}, u32[]{:S(2)}) collective-permute-start(bf16[512,2,256]{2,1,0:T(2,128)(2,1)} %get-tuple-element.23), channel_id=1, source_target_pairs={{0,20},{4,24},{8,28},{12,0},{16,4},{20,8},{24,12},{28,16},{1,21},{... | collective-permute-start | bytes 1572872 | tf_op jit(solution)/shard_map/ppermute | solution.py:220
  50.0 47.4 %collective-permute-start.5 = (bf16[512,2,256]{2,1,0:T(2,128)(2,1)}, bf16[512,2,256]{2,1,0:T(2,128)(2,1)}, u32[]{:S(2)}, u32[]{:S(2)}) collective-permute-start(bf16[512,2,256]{2,1,0:T(2,128)(2,1)} %get-tuple-element.29), channel_id=1, source_target_pairs={{0,24},{4,28},{8,0},{12,4},{16,8},{20,12},{24,16},{28,20},{1,25},{... | collective-permute-start | bytes 1572872 | tf_op jit(solution)/shard_map/ppermute | solution.py:220
  51.8 50.9 %collective-permute-start.6 = (bf16[512,2,256]{2,1,0:T(2,128)(2,1)}, bf16[512,2,256]{2,1,0:T(2,128)(2,1)}, u32[]{:S(2)}, u32[]{:S(2)}) collective-permute-start(bf16[512,2,256]{2,1,0:T(2,128)(2,1)} %get-tuple-element.22), channel_id=1, source_target_pairs={{0,28},{4,0},{8,4},{12,8},{16,12},{20,16},{24,20},{28,24},{1,29},{... | collective-permute-start | bytes 1572872 | tf_op jit(solution)/shard_map/ppermute | solution.py:220
  102.7 7.1 %copy-start.9 = (f32[3,256]{1,0:T(4,128)S(1)}, f32[3,256]{1,0:T(4,128)}, u32[]{:S(2)}) copy-start(f32[3,256]{1,0:T(4,128)} %param.22) | copy-start | bytes 9220
  102.7 7.1 %copy-start.11 = (f32[3]{0:T(128)S(1)}, f32[3]{0:T(128)}, u32[]{:S(2)}) copy-start(f32[3]{0:T(128)} %constant.148.clone) | copy-start | bytes 40
  113.7 1.2 copy-start.3
  148.4 48.3 %copy-start.6 = (f32[2,1024]{1,0:T(2,128)S(1)}, f32[2,1024]{1,0:T(2,128)}, u32[]{:S(2)}) copy-start(f32[2,1024]{1,0:T(2,128)} %param.29) | copy-start | bytes 24580
  148.4 48.3 %copy-start.7 = (f32[2,1024]{1,0:T(2,128)S(1)}, f32[2,1024]{1,0:T(2,128)}, u32[]{:S(2)}) copy-start(f32[2,1024]{1,0:T(2,128)} %param.30) | copy-start | bytes 24580
  148.4 57.6 %copy-start.5 = (f32[1024]{0:T(1024)S(1)}, f32[1024]{0:T(1024)}, u32[]{:S(2)}) copy-start(f32[1024]{0:T(1024)} %param.24) | copy-start | bytes 12292
  192.8 68.4 %copy-start.10 = (f32[1024]{0:T(1024)S(1)}, f32[1024]{0:T(1024)}, u32[]{:S(2)}) copy-start(f32[1024]{0:T(1024)} %param.26) | copy-start | bytes 12292
  192.8 12.4 %all-to-all-start = ((bf16[4,256,256]{1,2,0:T(8,128)(2,1)}), bf16[4,256,256]{1,2,0:T(8,128)(2,1)S(1)}, u32[]{:S(2)}, u32[]{:S(2)}) async-start(bf16[4,256,256]{1,2,0:T(8,128)(2,1)} %copy.25), calls=%async_computation | async-start | bytes 1048576 | tf_op jit(solution)/shard_map/all_to_all | solution.py:248
  196.4 64.8 %all-gather.7.cloned.1.call-start = ((), (), s32[]{:S(2)}) async-start(), calls=%async_computation.3 | async-start | bytes 2621440 | tf_op jit(solution)/shard_map/all_gather | solution.py:255
  205.2 0.8 copy-start.2
  210.0 111.8 %reduce-scatter.2.cloned.1.call-start = ((), (), s32[]{:S(2)}) async-start(), calls=%async_computation.4 | async-start | bytes 5242880 | tf_op jit(solution)/shard_map/reduce_scatter | solution.py:263
  277.0 44.8 %copy-start.4 = (f32[1024]{0:T(1024)S(1)}, f32[1024]{0:T(1024)}, u32[]{:S(2)}) copy-start(f32[1024]{0:T(1024)} %param.28) | copy-start | bytes 12292
  321.8 3.5 %copy-start.1 = (f32[256,1024]{1,0:T(8,128)S(1)}, f32[256,1024]{1,0:T(8,128)}, u32[]{:S(2)}) copy-start(f32[256,1024]{1,0:T(8,128)} %reduce-scatter.2.cloned.1.call-done) | copy-start | bytes 3145732
Sparse Core Ops, SparseCore 0:
  9.5 25.2 all-gather.8
  62.4 65.4 all-gather.4
  210.1 51.0 all-gather.6
  277.2 44.5 reduce-scatter.1
